TPU v7x, 256 devices: a whole 4x4x8 slice. The times are simulated.
256 devices in a mesh: rows: 64 (over y, z, core), freq: 4 (over x).
Axes of the slice: x: 4, y: 4, z: 8, core: 2. Of those that a mesh axis runs over, the one named last changes fastest.
Arguments:
- snapshots: bfloat16 [1048576, 512], P('rows', 'freq'), may hold values from -60 to 60
- block_cols: int32 [8192, 3], P('rows'), may hold values from 0 to 8191, as said below
- mass_blocks: bfloat16 [8192, 3, 128, 128], P('rows'), may hold values from -2 to 2
- start_group: float32 [512, 32], P('freq'), may hold values from -6 to 6
- start_merge: float32 [64, 32], replicated, may hold values from -6 to 6
Outputs:
- modes: float32 [32, 1048576], P(None, ('rows', 'freq'))
Inputs may be any that keep to these rules, and one draw needn't show every extreme that they name: block_cols[b, 0] is b; the other entries lie within 2 of b, differ from b, and may repeat near the ends.
All inputs are finite; a program needn't handle non-finite values.
Results may differ from a plain program's by a relative error of at most 0.0003.
Values may be sent and summed in bfloat16 or wider, within the bound.
No kernel may reach another device: no remote copies, remote signals or barrier semaphores. Data moves between devices by JAX's collectives and lax.ppermute only.
A program may use at most 128 MiB of HBM per device.

v0:
```python
import jax
import jax.numpy as jnp
from jax import lax
from jax.sharding import PartitionSpec as P

HB = 2
POWER = 2
HIGHEST = lax.Precision.HIGHEST


def extended_2(block, sides, width):
    for axis, dim in sides:
        count = lax.axis_size(axis)
        forward = [(i, i + 1) for i in range(count - 1)]
        backward = [(target, source) for source, target in forward]
        low = lax.ppermute(
            lax.slice_in_dim(block, block.shape[dim] - width, None, axis=dim), axis, forward
        )
        high = lax.ppermute(lax.slice_in_dim(block, 0, width, axis=dim), axis, backward)
        block = jnp.concatenate([low, block, high], axis=dim)
    return block


def orthonormal(columns_block):
    inner_gram = jnp.dot(columns_block.T, columns_block, precision=HIGHEST)
    lower_factor = jnp.linalg.cholesky(inner_gram)
    return lax.linalg.triangular_solve(
        lower_factor, columns_block, left_side=False, lower=True, transpose_a=True
    )


def subspace(gram_matrix, start_block):
    current = start_block
    for repeat in range(POWER):
        current = orthonormal(jnp.dot(gram_matrix, current, precision=HIGHEST))
    return current


def coefficient_tree(full_gram, start_merge, rank_size, freq_count):
    pairs = freq_count // 2
    width = 2 * rank_size
    blocks = jnp.stack(
        [full_gram[p * width : (p + 1) * width, p * width : (p + 1) * width] for p in range(pairs)]
    )
    pair_weights = jax.vmap(subspace, in_axes=(0, None))(blocks, start_merge)
    zero = jnp.zeros((width, rank_size), jnp.float32)
    coefficients = []
    for p in range(pairs):
        parts = [zero] * pairs
        parts[p] = pair_weights[p]
        coefficients.append(jnp.concatenate(parts, axis=0))
    while len(coefficients) > 1:
        merged = []
        for position in range(0, len(coefficients), 2):
            joined = jnp.concatenate([coefficients[position], coefficients[position + 1]], axis=1)
            pair_gram = jnp.dot(
                joined.T, jnp.dot(full_gram, joined, precision=HIGHEST), precision=HIGHEST
            )
            merged.append(jnp.dot(joined, subspace(pair_gram, start_merge), precision=HIGHEST))
        coefficients = merged
    return coefficients[0]


def shards(snapshots, block_cols, mass_blocks, start_group, start_merge):
    block_size = mass_blocks.shape[2]
    local_blocks = block_cols.shape[0]
    local_cols = snapshots.shape[1]
    total_rows = lax.axis_size("rows") * snapshots.shape[0]
    extended = extended_2(snapshots, (("rows", 0),), HB * block_size)
    tile_stack = extended.reshape(local_blocks + 2 * HB, block_size, local_cols)
    local_index = block_cols - lax.axis_index("rows") * local_blocks + HB
    picked = tile_stack[local_index]
    weighted = jnp.einsum("bkij,bkjc->bic", mass_blocks, picked, preferred_element_type=jnp.float32)
    weighted = weighted.reshape(local_blocks * block_size, local_cols)
    local_gram = jnp.dot(weighted.T, weighted, precision=HIGHEST)
    group_gram = lax.psum(local_gram, "rows") / total_rows
    weights = subspace(group_gram, start_group)
    modes = lax.dot_general(weights, weighted, (((0,), (1,)), ((), ())), precision=HIGHEST)
    rank_size = modes.shape[0]
    freq_count = lax.axis_size("freq")
    quarter = lax.all_to_all(modes, "freq", 1, 0, tiled=True)
    full_gram = (
        lax.psum(jnp.dot(quarter, quarter.T, precision=HIGHEST), ("rows", "freq")) / total_rows
    )
    combined = coefficient_tree(full_gram, start_merge, rank_size, freq_count)
    result = jnp.dot(combined.T, quarter, precision=HIGHEST)
    return result


def solution(mesh):
    in_specs = (
        P("rows", "freq"),
        P("rows", None),
        P("rows", None, None, None),
        P("freq", None),
        P(),
    )
    out_specs = P(None, ("rows", "freq"))
    return jax.shard_map(shards, mesh=mesh, in_specs=in_specs, out_specs=out_specs, check_vma=False)
```

profile of v0, /device:TPU:1, one launch (start us, length us, event | category | flops | bytes accessed | tf_op | source)
XLA Modules:
  0.0 596.8 jit_solution(17205891390755514347)
XLA Ops:
  7.4 4.9 collective-permute-start
  15.3 2.6 collective-permute-done.1
  18.0 10.8 %pad_maximum_fusion = bf16[16896,128]{1,0:T(8,128)(2,1)} fusion(bf16[256,128]{1,0:T(8,128)(2,1)S(1)} %collective-permute-done.1, bf16[16384,128]{1,0:T(8,128)(2,1)} %param.13, bf16[256,128]{1,0:T(8,128)(2,1)S(1)} %collective-permute-done), kind=kLoop, calls=%fused_computation.3 | loop fusion | flops 12976128 | bytes 8650752 | tf_op jit(solution)/shard_map/concatenate | solution.py:20
  28.7 13.6 %gather_fusion = bf16[384,128,128]{2,1,0:T(8,128)(2,1)} fusion(bf16[132,128,128]{2,1,0:T(8,128)(2,1)} %bitcast.133, s32[1024]{0:T(1024)S(1)} %pad_clamp_fusion), kind=kCustom, calls=%fused_computation | custom fusion | bytes 25167360 | tf_op jit(solution)/shard_map/gather | solution.py:72
  42.3 14.8 %fusion.62 = f32[128,128,128,1]{1,2,3,0:T(8,128)} fusion(bf16[128,3,128,128]{3,2,1,0:T(8,128)(2,1)} %param.15, bf16[128,3,128,128]{3,2,1,0:T(8,128)(2,1)} %bitcast.132), kind=kOutput, calls=%fused_computation.103 | convolution fusion | flops 1610612736 | bytes 33554432 | tf_op jit(solution)/shard_map/bkij,bkjc->bic/dot_general | solution.py:73
  57.1 17.6 %fusion.2 = f32[128,128]{1,0:T(8,128)} fusion(f32[128,128,128,1]{1,2,3,0:T(8,128)} %fusion.62), kind=kOutput, calls=%fused_computation.4 | convolution fusion | flops 3221225472 | bytes 8454144 | tf_op jit(solution)/shard_map/dot_general | solution.py:75
  74.7 173.3 %all-reduce.5.cloned.1.call-done = f32[128,128]{1,0:T(8,128)} async-done(((f32[128,128]{1,0:T(8,128)}), f32[128,128]{1,0:T(8,128)}) %all-reduce.5.cloned.1.call-update) | async-done | bytes 65552 | tf_op jit(solution)/shard_map/psum | solution.py:76
  249.3 2.9 cholesky.117
  253.6 2.4 custom-call.18
  257.6 2.9 cholesky.128
  261.8 2.4 custom-call.19
  264.5 13.0 %fusion.53 = f32[32,4,4096]{2,0,1:T(8,128)} fusion(f32[128,32,1]{0,1,2:T(8,128)S(1)} %convolution_bitcast_fusion.4, f32[4,4096,128]{2,1,0:T(8,128)} %bitcast.131), kind=kOutput, calls=%fused_computation.94 | convolution fusion | flops 805306368 | bytes 10502144 | tf_op jit(solution)/shard_map/dot_general | solution.py:78
  277.5 4.0 all-to-all-start
  281.5 25.8 %all-to-all-done = f32[32,4,4096]{2,0,1:T(8,128)S(1)} async-done(((f32[32,4,4096]{2,0,1:T(8,128)}), f32[32,4,4096]{2,0,1:T(8,128)S(1)}, u32[]{:S(2)}, u32[]{:S(2)}) %all-to-all-start) | async-done | bytes 2097184 | tf_op jit(solution)/shard_map/all_to_all | solution.py:81
  307.2 2.4 fusion.54
  309.7 237.2 %all-reduce.7.cloned.1.call-done = f32[128,128]{1,0:T(8,128)} async-done(((f32[128,128]{1,0:T(8,128)}), f32[128,128]{1,0:T(8,128)}) %all-reduce.7.cloned.1.call-update) | async-done | bytes 65552 | tf_op jit(solution)/shard_map/psum | solution.py:83
  548.4 6.1 %custom-call.20 = f32[2,32,32]{2,1,0:T(8,128)S(1)} custom-call(f32[2,32,32]{2,1,0:T(8,128)S(1)} %fusion.14), custom_call_target="Cholesky" | custom-call | tf_op jit(solution)/shard_map/vmap(jit(cholesky))/cholesky | solution.py:26
  554.8 4.9 custom-call.21
  560.5 5.9 custom-call.22
  566.6 4.9 custom-call.23
  573.5 2.9 cholesky.161
  577.8 2.4 custom-call.24
  580.9 2.9 cholesky.172
  585.1 2.4 custom-call.25
  (72 shorter events, 19.9 us)
Async XLA Ops:
  6.5 541.3 %copy-start = (f32[64,32]{0,1:T(8,128)S(1)}, f32[64,32]{0,1:T(8,128)}, u32[]{:S(2)}) copy-start(f32[64,32]{0,1:T(8,128)} %param.17) | copy-start | bytes 24580
  6.5 241.5 %all-reduce.5.cloned.1.call-start = ((), (), s32[]{:S(2)}) async-start(), calls=%async_computation.1 | async-start | bytes 131072 | tf_op jit(solution)/shard_map/psum | solution.py:76
  7.4 7.9 %collective-permute-start = (bf16[256,128]{1,0:T(8,128)(2,1)S(1)}, bf16[256,128]{1,0:T(8,128)(2,1)S(1)}, u32[]{:S(2)}, u32[]{:S(2)}) collective-permute-start(bf16[256,128]{1,0:T(8,128)(2,1)S(1)} %get-tuple-element.6), channel_id=1, source_target_pairs={{0,4},{4,8},{8,12},{12,16},{16,20},{20,24},{24,28},{28,32},{32,36}... | collective-permute-start | bytes 196616 | tf_op jit(solution)/shard_map/ppermute | solution.py:16
  12.4 5.6 collective-permute-start.1
  57.1 191.0 %copy-start.1 = (f32[128,32]{0,1:T(8,128)S(1)}, f32[128,32]{0,1:T(8,128)}, u32[]{:S(2)}) copy-start(f32[128,32]{0,1:T(8,128)} %param.16) | copy-start | bytes 49156
  277.5 29.7 %all-to-all-start = ((f32[32,4,4096]{2,0,1:T(8,128)}), f32[32,4,4096]{2,0,1:T(8,128)S(1)}, u32[]{:S(2)}, u32[]{:S(2)}) async-start(f32[32,4,4096]{2,0,1:T(8,128)} %fusion.53), calls=%async_computation | async-start | bytes 4194304 | tf_op jit(solution)/shard_map/all_to_all | solution.py:81
  281.5 265.5 %all-reduce.7.cloned.1.call-start = ((), (), s32[]{:S(2)}) async-start(), calls=%async_computation.2 | async-start | bytes 131072 | tf_op jit(solution)/shard_map/psum | solution.py:83
Sparse Core Ops, SparseCore 0:
  74.8 173.1 all-reduce.4
  309.8 237.0 all-reduce.6
where the time goes:
time: 597 us
  waiting for transfers between devices  439 us (74%)
  other arithmetic  61.4 us (10%)
  matrix products  56.6 us (9%)
  local copies, waits for them, and re-layouts  15.3 us (3%)
  between operations  13.7 us (2%)
  starting transfers between devices  10.8 us (2%)
    psum x1, waiting for transfers between devices, shards(): lax.psum(jnp.dot(quarter, quarter.T, precision=HIGHEST), ('rows', 'freq'))  237 us
    psum x1, waiting for transfers between devices, shards(): group_gram = lax.psum(local_gram, 'rows') / total_rows  173 us
    another operation x19, other arithmetic, orthonormal(): lower_factor = jnp.linalg.cholesky(inner_gram)  26.7 us
    all_to_all x1, waiting for transfers between devices, shards(): quarter = lax.all_to_all(modes, 'freq', 1, 0, tiled=True)  25.8 us
    another operation x13, other arithmetic, orthonormal(): lax.linalg.triangular_solve(lower_factor, columns_block, left_side=False,...  22.3 us
    dot_general x1, matrix products, shards(): local_gram = jnp.dot(weighted.T, weighted, precision=HIGHEST)  17.6 us
    dot_general x1, matrix products, shards(): jnp.einsum('bkij,bkjc->bic', mass_blocks, picked, preferred_element_type=...  14.8 us
    gather x1, local copies, waits for them, and re-layouts, shards(): picked = tile_stack[local_index]  13.6 us
  transfers between devices with their start and end apart: 5, of which 4 were waited for; matrix products, arithmetic and copies ran while one was open for 0% of the time, Pallas kernels for 0%

commit v1 on v0

--- a/solution.py
+++ b/solution.py
@@ -80,7 +80,10 @@
     freq_count = lax.axis_size("freq")
     quarter = lax.all_to_all(modes, "freq", 1, 0, tiled=True)
     full_gram = (
-        lax.psum(jnp.dot(quarter, quarter.T, precision=HIGHEST), ("rows", "freq")) / total_rows
+        jnp.sum(
+            lax.all_gather(jnp.dot(quarter, quarter.T, precision=HIGHEST), ("rows", "freq")), axis=0
+        )
+        / total_rows
     )
     combined = coefficient_tree(full_gram, start_merge, rank_size, freq_count)
     result = jnp.dot(combined.T, quarter, precision=HIGHEST)

time: 597 us -> 483 us (0.81)
  waiting for transfers between devices: 439 us -> 297 us
  blocking collectives: 0 us -> 29.2 us
    psum x1 -> x0, waiting for transfers between devices: 237 us -> none  [shards(): lax.psum(jnp.dot(quarter, quarter.T, precision=HIGHEST), ('rows', 'freq'))]
    all_gather x0 -> x1, waiting for transfers between devices: none -> 121 us  [shards(): lax.all_gather(jnp.dot(quarter, quarter.T, precision=HIGHEST), ('rows', '...]
    all_to_all x0 -> x1, blocking collectives: none -> 29.2 us  [shards(): quarter = lax.all_to_all(modes, 'freq', 1, 0, tiled=True)]
    all_to_all x1 -> x0, waiting for transfers between devices: 25.8 us -> none  [shards(): quarter = lax.all_to_all(modes, 'freq', 1, 0, tiled=True)]
    reduce_sum x0 -> x1, other arithmetic: none -> 6.59 us  [shards(): jnp.sum(lax.all_gather(jnp.dot(quarter, quarter.T, precision=HIGHEST), ('...]
  transfers between devices with their start and end apart: 5 -> 4, of which waited for: 4 -> 3; matrix products, arithmetic and copies ran while one was open for 0% -> 0% of each run, Pallas kernels for 0% -> 0%
where the time goes in v1:
time: 483 us
  waiting for transfers between devices  297 us (61%)
  other arithmetic  66.9 us (14%)
  matrix products  53.5 us (11%)
  blocking collectives  29.2 us (6%)
  local copies, waits for them, and re-layouts  15.3 us (3%)
  between operations  13.7 us (3%)
  starting transfers between devices  6.89 us (1%)
    psum x1, waiting for transfers between devices, shards(): group_gram = lax.psum(local_gram, 'rows') / total_rows  173 us
    all_gather x1, waiting for transfers between devices, shards(): lax.all_gather(jnp.dot(quarter, quarter.T, precision=HIGHEST), ('rows', '...  121 us
    all_to_all x1, blocking collectives, shards(): quarter = lax.all_to_all(modes, 'freq', 1, 0, tiled=True)  29.2 us
    another operation x19, other arithmetic, orthonormal(): lower_factor = jnp.linalg.cholesky(inner_gram)  26.4 us
    another operation x13, other arithmetic, orthonormal(): lax.linalg.triangular_solve(lower_factor, columns_block, left_side=False,...  22.3 us
    dot_general x1, matrix products, shards(): local_gram = jnp.dot(weighted.T, weighted, precision=HIGHEST)  17.6 us
    dot_general x1, matrix products, shards(): jnp.einsum('bkij,bkjc->bic', mass_blocks, picked, preferred_element_type=...  14.8 us
    gather x1, local copies, waits for them, and re-layouts, shards(): picked = tile_stack[local_index]  13.6 us
  transfers between devices with their start and end apart: 4, of which 3 were waited for; matrix products, arithmetic and copies ran while one was open for 0% of the time, Pallas kernels for 0%

profile of v1, /device:TPU:1, one launch (start us, length us, event | category | flops | bytes accessed | tf_op | source)
XLA Modules:
  0.0 482.8 jit_solution(7609455857864870101)
XLA Ops:
  7.4 4.9 %collective-permute-start = (bf16[256,128]{1,0:T(8,128)(2,1)S(1)}, bf16[256,128]{1,0:T(8,128)(2,1)S(1)}, u32[]{:S(2)}, u32[]{:S(2)}) collective-permute-start(bf16[256,128]{1,0:T(8,128)(2,1)S(1)} %get-tuple-element.6), channel_id=1, source_target_pairs={{0,4},{4,8},{8,12},{12,16},{16,20},{20,24},{24,28},{28,32},{32,36}... | collective-permute-start | bytes 196616 | tf_op jit(solution)/shard_map/ppermute | solution.py:16
  15.3 2.6 collective-permute-done.1
  18.0 10.8 %pad_maximum_fusion = bf16[16896,128]{1,0:T(8,128)(2,1)} fusion(bf16[256,128]{1,0:T(8,128)(2,1)S(1)} %collective-permute-done.1, bf16[16384,128]{1,0:T(8,128)(2,1)} %param.13, bf16[256,128]{1,0:T(8,128)(2,1)S(1)} %collective-permute-done), kind=kLoop, calls=%fused_computation.3 | loop fusion | flops 12976128 | bytes 8650752 | tf_op jit(solution)/shard_map/concatenate | solution.py:20
  28.7 13.6 %gather_fusion = bf16[384,128,128]{2,1,0:T(8,128)(2,1)} fusion(bf16[132,128,128]{2,1,0:T(8,128)(2,1)} %bitcast.134, s32[1024]{0:T(1024)S(1)} %pad_clamp_fusion), kind=kCustom, calls=%fused_computation | custom fusion | bytes 25167360 | tf_op jit(solution)/shard_map/gather | solution.py:72
  42.3 14.8 %fusion.62 = f32[128,128,128,1]{1,2,3,0:T(8,128)} fusion(bf16[128,3,128,128]{3,2,1,0:T(8,128)(2,1)} %param.15, bf16[128,3,128,128]{3,2,1,0:T(8,128)(2,1)} %bitcast.133), kind=kOutput, calls=%fused_computation.103 | convolution fusion | flops 1610612736 | bytes 33554432 | tf_op jit(solution)/shard_map/bkij,bkjc->bic/dot_general | solution.py:73
  57.1 17.6 %fusion.2 = f32[128,128]{1,0:T(8,128)} fusion(f32[128,128,128,1]{1,2,3,0:T(8,128)} %fusion.62), kind=kOutput, calls=%fused_computation.4 | convolution fusion | flops 3221225472 | bytes 8454144 | tf_op jit(solution)/shard_map/dot_general | solution.py:75
  74.7 173.3 %all-reduce.4.cloned.1.call-done = f32[128,128]{1,0:T(8,128)} async-done(((f32[128,128]{1,0:T(8,128)}), f32[128,128]{1,0:T(8,128)}) %all-reduce.4.cloned.1.call-update) | async-done | bytes 65552 | tf_op jit(solution)/shard_map/psum | solution.py:76
  249.3 2.9 cholesky.117
  253.6 2.4 custom-call.18
  257.6 2.9 cholesky.128
  261.8 2.4 custom-call.19
  264.5 10.7 %fusion.53 = f32[32,4,4096]{2,0,1:T(8,128)S(1)} fusion(f32[128,32,1]{0,1,2:T(8,128)S(1)} %convolution_bitcast_fusion.4, f32[4,4096,128]{2,1,0:T(8,128)} %bitcast.132), kind=kOutput, calls=%fused_computation.94 | convolution fusion | flops 805306368 | bytes 10502144 | tf_op jit(solution)/shard_map/dot_general | solution.py:78
  275.2 29.2 %all_to_all.16 = f32[32,4,4096]{2,0,1:T(8,128)S(1)} all-to-all(f32[32,4,4096]{2,0,1:T(8,128)S(1)} %fusion.53), channel_id=1, replica_groups=mesh['rows'=64,'freq'=4] {'freq'}, dimensions={1} | all-to-all | bytes 4194304 | tf_op jit(solution)/shard_map/all_to_all | solution.py:81
  304.4 2.4 fusion.54
  306.9 121.4 %all-gather.3.cloned.1.call-done = f32[32768,128]{1,0:T(8,128)} async-done(((f32[128,128]{1,0:T(8,128)}), f32[32768,128]{1,0:T(8,128)}) %all-gather.3.cloned.1.call-update) | async-done | bytes 16777232 | tf_op jit(solution)/shard_map/all_gather | solution.py:84
  428.3 6.6 %reduce_sum.9 = f32[128,128]{1,0:T(8,128)S(1)} reduce(f32[256,128,128]{2,1,0:T(8,128)} %bitcast.137, f32[]{:T(128)} %constant.83.clone.1), dimensions={0}, to_apply=%region_3.6 | reduce | flops 4177920 | bytes 16842756 | tf_op jit(solution)/shard_map/reduce_sum | solution.py:83
  435.5 5.9 %custom-call.20 = f32[2,32,32]{2,1,0:T(8,128)S(1)} custom-call(f32[2,32,32]{2,1,0:T(8,128)S(1)} %fusion.14), custom_call_target="Cholesky" | custom-call | tf_op jit(solution)/shard_map/vmap(jit(cholesky))/cholesky | solution.py:26
  441.6 4.9 %custom-call.21 = f32[2,1,32,32]{2,3,1,0:T(8,128)S(1)} custom-call(f32[2,1,32,32]{3,2,1,0:T(8,128)S(1)} %select_bitcast_fusion.1), custom_call_target="InvertDiagBlocksLowerTriangular" | custom-call | tf_op jit(solution)/shard_map/vmap()/triangular_solve/custom-call.3 | solution.py:27
  447.3 5.9 %custom-call.22 = f32[2,32,32]{2,1,0:T(8,128)S(1)} custom-call(f32[2,32,32]{2,1,0:T(8,128)S(1)} %fusion.12), custom_call_target="Cholesky" | custom-call | tf_op jit(solution)/shard_map/vmap(jit(cholesky))/cholesky | solution.py:26
  453.4 4.9 %custom-call.23 = f32[2,1,32,32]{2,3,1,0:T(8,128)S(1)} custom-call(f32[2,1,32,32]{3,2,1,0:T(8,128)S(1)} %select_bitcast_fusion), custom_call_target="InvertDiagBlocksLowerTriangular" | custom-call | tf_op jit(solution)/shard_map/vmap()/triangular_solve/custom-call.3 | solution.py:27
  459.5 2.9 cholesky.161
  463.8 2.4 custom-call.24
  466.9 2.9 cholesky.172
  471.1 2.4 custom-call.25
  (72 shorter events, 18.3 us)
Async XLA Ops:
  6.5 428.4 %copy-start = (f32[64,32]{0,1:T(8,128)S(1)}, f32[64,32]{0,1:T(8,128)}, u32[]{:S(2)}) copy-start(f32[64,32]{0,1:T(8,128)} %param.17) | copy-start | bytes 24580
  6.5 241.5 %all-reduce.4.cloned.1.call-start = ((), (), s32[]{:S(2)}) async-start(), calls=%async_computation.1 | async-start | bytes 131072 | tf_op jit(solution)/shard_map/psum | solution.py:76
  7.4 7.9 %collective-permute-start = (bf16[256,128]{1,0:T(8,128)(2,1)S(1)}, bf16[256,128]{1,0:T(8,128)(2,1)S(1)}, u32[]{:S(2)}, u32[]{:S(2)}) collective-permute-start(bf16[256,128]{1,0:T(8,128)(2,1)S(1)} %get-tuple-element.6), channel_id=1, source_target_pairs={{0,4},{4,8},{8,12},{12,16},{16,20},{20,24},{24,28},{28,32},{32,36}... | collective-permute-start | bytes 196616 | tf_op jit(solution)/shard_map/ppermute | solution.py:16
  12.4 5.6 %collective-permute-start.1 = (bf16[256,128]{1,0:T(8,128)(2,1)S(1)}, bf16[256,128]{1,0:T(8,128)(2,1)S(1)}, u32[]{:S(2)}, u32[]{:S(2)}) collective-permute-start(bf16[256,128]{1,0:T(8,128)(2,1)S(1)} %get-tuple-element.8), channel_id=1, source_target_pairs={{4,0},{8,4},{12,8},{16,12},{20,16},{24,20},{28,24},{32,28},{36,32}... | collective-permute-start | bytes 196616 | tf_op jit(solution)/shard_map/ppermute | solution.py:19
  57.1 191.0 %copy-start.1 = (f32[128,32]{0,1:T(8,128)S(1)}, f32[128,32]{0,1:T(8,128)}, u32[]{:S(2)}) copy-start(f32[128,32]{0,1:T(8,128)} %param.16) | copy-start | bytes 49156
  74.7 353.6 %all-gather.3.cloned.1.call-start = ((), (), s32[]{:S(2)}) async-start(), calls=%async_computation.2 | async-start | bytes 16842752 | tf_op jit(solution)/shard_map/all_gather | solution.py:84
Sparse Core Ops, SparseCore 0:
  74.8 173.1 all-reduce.3
  307.0 121.2 all-gather.2
